TPU v7x, 256 devices: a whole 4x4x8 slice. The times are simulated.
256 devices in a mesh: cfg: 2 (over z_lo), seq: 16 (over z_hi, x), wblk: 8 (over y, core).
Axes of the slice: x: 4, y: 4, z: 8 (z_hi: 4, z_lo: 2; z = z_hi * 2 + z_lo), core: 2. Of those that a mesh axis runs over, the one named last changes fastest.
Arguments:
- text_tokens: bfloat16 [2, 2, 512, 3072], P('cfg', None, 'seq', 'wblk'), may hold values from -16 to 16
- image_tokens: bfloat16 [2, 4096, 3072], P(None, 'seq', 'wblk'), may hold values from -16 to 16
- pooled_vector: float32 [2, 3072], P('cfg', 'seq'), may hold values from -6 to 6
- mod_weight: bfloat16 [3072, 3, 3072], P('seq', None, 'wblk'), may hold values from -0.109375 to 0.109375
- qkv_weight: bfloat16 [3072, 3, 16, 128], P('seq', None, 'wblk'), may hold values from -0.109375 to 0.109375
- up_weight: bfloat16 [3072, 6144], P('seq', 'wblk'), may hold values from -0.109375 to 0.109375
- query_gain: float32 [128], replicated, may hold values from 0.6 to 10
- key_gain: float32 [128], replicated, may hold values from 0.6 to 10
- attn_weight: bfloat16 [2048, 3072], P('wblk', 'seq'), may hold values from -0.125 to 0.125
- down_weight: bfloat16 [6144, 3072], P('wblk', 'seq'), may hold values from -0.078125 to 0.078125
- lengths: int32 [2], replicated, may hold values from 1 to 512, as said below
- timestep: int32 [1], replicated, may hold values from 0 to 27
Outputs:
- text_out: bfloat16 [2, 2, 512, 3072], P('cfg', None, 'seq', 'wblk')
- velocity: float32 [2, 4096, 3072], P('cfg', 'seq', 'wblk')
- new_image: float32 [2, 4096, 3072], P('cfg', 'seq', 'wblk')
Inputs may be any that keep to these rules, and one draw needn't show every extreme that they name: `lengths`: some prompt has all 512 text tokens live in every draw.
All inputs are finite; a program needn't handle non-finite values.
Results may differ from a plain program's by a relative error of at most 0.025.
Values may be sent and summed in bfloat16 or wider, within the bound.
No kernel may reach another device: no remote copies, remote signals or barrier semaphores. Data moves between devices by JAX's collectives and lax.ppermute only.
A program may use at most 128 MiB of HBM per device.

v0:
```python
import math
import jax
import jax.numpy as jnp
from jax import lax
from jax.sharding import PartitionSpec as P

D = 3072
HD = 128
GRID = 64
STEPS = 28
epsilon = 1e-06
guidance = 3.5
time_shift = 3.0
rope_theta = 10000.0


def plan(timestep):
    step_index = timestep[0].astype(jnp.float32)
    time_now = 1.0 - step_index / STEPS
    time_next = 1.0 - (step_index + 1.0) / STEPS
    sigma_now = time_shift * time_now / (1.0 + (time_shift - 1.0) * time_now)
    sigma_next = time_shift * time_next / (1.0 + (time_shift - 1.0) * time_next)
    return (sigma_now, sigma_next - sigma_now)


def time_embedding(sigma_now, dim_count):
    halfwidth = dim_count // 2
    frequency = jnp.exp(-math.log(10000.0) * jnp.arange(halfwidth, dtype=jnp.float32) / halfwidth)
    angles = 1000.0 * sigma_now * frequency
    return jnp.concatenate([jnp.cos(angles), jnp.sin(angles)])


def inverse_freq(dim_count):
    return rope_theta ** (-jnp.arange(0, dim_count, 2, dtype=jnp.float32) / dim_count)


def rotary_angles(height_pos, width_pos):
    still_dims = HD // 8
    axis_dims = (HD - still_dims) // 2
    return jnp.concatenate(
        [
            jnp.zeros((height_pos.shape[0], still_dims // 2), jnp.float32),
            height_pos[:, None] * inverse_freq(axis_dims)[None],
            width_pos[:, None] * inverse_freq(axis_dims)[None],
        ],
        axis=1,
    )


def rotate(vectors, angles):
    paired_dims = vectors.reshape(vectors.shape[:-1] + (HD // 2, 2))
    cosine_table = jnp.cos(angles)[:, None, :]
    sine_table = jnp.sin(angles)[:, None, :]
    first_part = paired_dims[..., 0]
    second_part = paired_dims[..., 1]
    turned = jnp.stack(
        [
            first_part * cosine_table - second_part * sine_table,
            first_part * sine_table + second_part * cosine_table,
        ],
        axis=-1,
    )
    return turned.reshape(vectors.shape)


def head_norm(vectors, gain_vector):
    return (
        vectors
        * lax.rsqrt(jnp.mean(vectors * vectors, axis=-1, keepdims=True) + epsilon)
        * gain_vector
    )


def input_folder(source, pieces):
    width_rows = pieces[0].shape[0]
    first_total = jnp.dot(
        source, pieces[0].reshape(width_rows, -1), preferred_element_type=jnp.float32
    )
    second_total = jnp.dot(source, pieces[1], preferred_element_type=jnp.float32)
    return (first_total, second_total)


def output_folder(attended, activated, pieces):
    block_cols = jnp.dot(attended, pieces[0], preferred_element_type=jnp.float32)
    block_cols = block_cols + jnp.dot(activated, pieces[1], preferred_element_type=jnp.float32)
    return block_cols


def shards(
    text_tokens,
    image_tokens,
    pooled_vector,
    mod_weight,
    qkv_weight,
    up_weight,
    query_gain,
    key_gain,
    attn_weight,
    down_weight,
    lengths,
    timestep,
):
    seq_pos = lax.axis_index("seq")
    cfg_pos = lax.axis_index("cfg")
    prompts = image_tokens.shape[0]
    image_rows = image_tokens.shape[1]
    text_rows = text_tokens.shape[2]
    local_len = text_rows + image_rows
    dim_local = image_tokens.shape[2]
    dim_seq = pooled_vector.shape[1]
    heads_local = qkv_weight.shape[2]
    row_count = prompts * local_len
    sigma_now, step_size = plan(timestep)
    embedded = lax.dynamic_slice_in_dim(time_embedding(sigma_now, D), seq_pos * dim_seq, dim_seq)
    cond_vec = jax.nn.silu(pooled_vector[0] + embedded).astype(jnp.bfloat16)[None]
    mod_terms = jnp.dot(
        cond_vec, mod_weight.reshape(dim_seq, 3 * dim_local), preferred_element_type=jnp.float32
    )
    modulation = lax.psum(mod_terms.reshape(3, dim_local), "seq")
    local_rows = jnp.concatenate([text_tokens[0], image_tokens], axis=1)
    hidden = local_rows.astype(jnp.float32)
    totals, squares = lax.psum(
        (jnp.sum(hidden, axis=-1), jnp.sum(hidden * hidden, axis=-1)), "wblk"
    )
    average = (totals / D)[..., None]
    variance = (squares / D)[..., None] - average * average
    normed = (
        (hidden - average) * lax.rsqrt(variance + epsilon) * (1.0 + modulation[1]) + modulation[0]
    ).astype(jnp.bfloat16)
    gathered = lax.all_gather(normed, "wblk", axis=2, tiled=True)
    token_rows = gathered.reshape(row_count, D)
    projected, mlp_units = input_folder(
        token_rows,
        (
            lax.all_gather(qkv_weight, "seq", axis=0, tiled=True),
            lax.all_gather(up_weight, "seq", axis=0, tiled=True),
        ),
    )
    projected = projected.reshape(prompts, local_len, 3, heads_local, HD)
    image_index = seq_pos * image_rows + jnp.arange(image_rows, dtype=jnp.int32)
    height_pos = jnp.concatenate(
        [jnp.zeros((text_rows,), jnp.float32), (image_index // GRID).astype(jnp.float32)]
    )
    width_pos = jnp.concatenate(
        [jnp.zeros((text_rows,), jnp.float32), (image_index % GRID).astype(jnp.float32)]
    )
    angles = rotary_angles(height_pos, width_pos)
    queries = rotate(head_norm(projected[:, :, 0], query_gain), angles).astype(jnp.bfloat16)
    key_rows = rotate(head_norm(projected[:, :, 1], key_gain), angles).astype(jnp.bfloat16)
    values = projected[:, :, 2].astype(jnp.bfloat16)
    scale_factor = HD ** (-0.5)
    seq_count = lax.psum(1, "seq")
    pair_count = prompts * heads_local
    subs = seq_count // pair_count
    sub_rows = local_len // subs
    pair_keys = key_rows.transpose(0, 2, 1, 3).reshape(pair_count, local_len, HD)
    pair_values = values.transpose(0, 2, 1, 3).reshape(pair_count, local_len, HD)
    pair_queries = queries.transpose(0, 2, 1, 3).reshape(seq_count, sub_rows, HD)
    send = jnp.concatenate(
        [
            jnp.broadcast_to(pair_keys[:, None], (pair_count, subs, local_len, HD)).reshape(
                seq_count, local_len, HD
            ),
            jnp.broadcast_to(pair_values[:, None], (pair_count, subs, local_len, HD)).reshape(
                seq_count, local_len, HD
            ),
            pair_queries,
        ],
        axis=1,
    )
    received = lax.all_to_all(send, "seq", 0, 0, tiled=True)
    key_piece = received[:, :local_len].reshape(seq_count * local_len, HD)
    value_piece = received[:, local_len : 2 * local_len].reshape(seq_count * local_len, HD)
    query_piece = received[:, 2 * local_len :].reshape(seq_count * sub_rows, HD)
    my_prompt = seq_pos // subs // heads_local
    width_keys = key_piece.shape[0]
    where_global = jnp.arange(width_keys, dtype=jnp.int32)
    shard_index = where_global // local_len
    within = where_global % local_len
    text_index = shard_index * text_rows + within
    key_live = (within >= text_rows) | (text_index < lengths[my_prompt])
    scores = jnp.dot(query_piece, key_piece.T, preferred_element_type=jnp.float32) * scale_factor
    scores = jnp.where(key_live[None, :], scores, -1e30)
    top_score = jnp.max(scores, axis=-1, keepdims=True)
    weights = jnp.exp(scores - top_score)
    denominator = jnp.sum(weights, axis=-1, keepdims=True)
    numerator = jnp.dot(
        weights.astype(jnp.bfloat16), value_piece, preferred_element_type=jnp.float32
    )
    mixed = (numerator / denominator).astype(jnp.bfloat16).reshape(seq_count, sub_rows, HD)
    returned = lax.all_to_all(mixed, "seq", 0, 0, tiled=True)
    attended = returned.reshape(prompts, heads_local, local_len, HD)
    attended = attended.transpose(0, 2, 1, 3).reshape(row_count, heads_local * HD)
    activated = jax.nn.gelu(mlp_units, approximate=True).astype(jnp.bfloat16)
    branch_terms = output_folder(
        attended,
        activated,
        (
            lax.all_gather(attn_weight, "seq", axis=1, tiled=True),
            lax.all_gather(down_weight, "seq", axis=1, tiled=True),
        ),
    )
    branch = lax.psum_scatter(
        branch_terms.reshape(prompts, local_len, D).astype(jnp.bfloat16),
        "wblk",
        scatter_dimension=2,
        tiled=True,
    ).astype(jnp.float32)
    layer_out = hidden + modulation[2] * branch
    text_out = layer_out[:, :text_rows].astype(jnp.bfloat16)[None]
    image_out = layer_out[:, text_rows:]
    paired = lax.all_to_all(
        image_out[:, None].astype(jnp.bfloat16), "cfg", split_axis=0, concat_axis=1, tiled=True
    ).astype(jnp.float32)
    velocity = paired[:, 1] + guidance * (paired[:, 0] - paired[:, 1])
    own_prompts = prompts // 2
    latent = lax.dynamic_slice_in_dim(image_tokens, cfg_pos * own_prompts, own_prompts, 0).astype(
        jnp.float32
    )
    new_image = latent + step_size * velocity
    return (text_out, velocity, new_image)


def solution(mesh):
    in_specs = (
        P("cfg", None, "seq", "wblk"),
        P(None, "seq", "wblk"),
        P("cfg", "seq"),
        P("seq", None, "wblk"),
        P("seq", None, "wblk", None),
        P("seq", "wblk"),
        P(),
        P(),
        P("wblk", "seq"),
        P("wblk", "seq"),
        P(),
        P(),
    )
    out_specs = (P("cfg", None, "seq", "wblk"), P("cfg", "seq", "wblk"), P("cfg", "seq", "wblk"))
    return jax.shard_map(shards, mesh=mesh, in_specs=in_specs, out_specs=out_specs, check_vma=False)
```

profile of v0, /device:TPU:2, one launch (start us, length us, event | category | flops | bytes accessed | tf_op | source)
XLA Modules:
  0.0 486.1 jit_solution(3172526040136737661)
XLA Ops:
  8.7 0.8 fusion.63
  9.7 1.3 convert_reduce_fusion
  11.0 15.1 %all-reduce.2 = (f32[2,288]{1,0:T(2,128)S(1)}, f32[2,288]{1,0:T(2,128)S(1)}) all-reduce(f32[2,288]{1,0:T(2,128)S(1)} %get-tuple-element.6, f32[2,288]{1,0:T(2,128)S(1)} %get-tuple-element.5), channel_id=1, replica_groups=mesh['cfg'=2,'seq'=16,'wblk'=8] {'wblk'}, use_global_device_ids=true, to_apply=%region_4.5 | all-reduce | flops 1152 | bytes 9216 | tf_op jit(solution)/shard_map/psum | solution.py:122
  26.1 46.3 %psum.21 = f32[3,384]{1,0:T(4,128)S(1)} all-reduce(f32[3,384]{1,0:T(4,128)S(1)} %bitcast.121), channel_id=1, replica_groups=mesh['cfg'=2,'seq'=16,'wblk'=8] {'seq'}, use_global_device_ids=true, to_apply=%region_0.1 | all-reduce | flops 1152 | bytes 9216 | tf_op jit(solution)/shard_map/psum | solution.py:119
  72.5 2.0 fusion.26
  75.8 0.8 mul.324
  76.6 0.8 mul.305
  78.1 13.8 %all-gather.8.cloned.1.call-done = bf16[3072,3,2,128]{3,2,1,0:T(2,128)(2,1)} async-done(((bf16[192,3,2,128]{3,2,1,0:T(2,128)(2,1)}), bf16[3072,3,2,128]{3,2,1,0:T(2,128)(2,1)}) %all-gather.8.cloned.1.call-update) | async-done | bytes 4718608 | tf_op jit(solution)/shard_map/all_gather | solution.py:135
  91.9 12.4 %copy.38 = bf16[3072,3,2,128]{0,3,2,1:T(8,128)(2,1)} copy(bf16[3072,3,2,128]{3,2,1,0:T(2,128)(2,1)} %all-gather.8.cloned.1.call-done) | data formatting | bytes 9437184 | tf_op jit(solution)/shard_map/reshape | solution.py:77
  104.3 23.6 %all-gather.6.cloned.1.call-done = bf16[2,288,3072]{2,1,0:T(8,128)(2,1)} async-done(((bf16[2,288,384]{2,1,0:T(8,128)(2,1)}), bf16[2,288,3072]{2,1,0:T(8,128)(2,1)}) %all-gather.6.cloned.1.call-update) | async-done | bytes 3538960 | tf_op jit(solution)/shard_map/all_gather | solution.py:130
  127.9 6.8 %fusion.6 = f32[2,288,3,2,128]{4,1,3,2,0:T(8,128)S(1)} fusion(bf16[3072,3,2,128]{0,3,2,1:T(8,128)(2,1)} %copy.38, bf16[2,288,3072]{2,1,0:T(8,128)(2,1)} %all-gather.6.cloned.1.call-done), kind=kOutput, calls=%fused_computation.8 | convolution fusion | flops 2717908992 | bytes 10027008 | tf_op jit(solution)/shard_map/dot_general | solution.py:76
  137.0 0.8 subtract_convert_fusion.1
  140.3 1.7 pad_maximum_fusion
  142.0 10.1 %all-to-all-start = ((bf16[16,648,128]{2,1,0:T(8,128)(2,1)}), bf16[16,648,128]{2,1,0:T(8,128)(2,1)S(1)}, u32[]{:S(2)}, u32[]{:S(2)}) async-start(bf16[16,648,128]{2,1,0:T(8,128)(2,1)} %pad_maximum_fusion), calls=%async_computation | async-start | bytes 5308416 | tf_op jit(solution)/shard_map/all_to_all | solution.py:171
  154.0 100.2 %all-to-all-done = bf16[16,648,128]{2,1,0:T(8,128)(2,1)S(1)} async-done(((bf16[16,648,128]{2,1,0:T(8,128)(2,1)}), bf16[16,648,128]{2,1,0:T(8,128)(2,1)S(1)}, u32[]{:S(2)}, u32[]{:S(2)}) %all-to-all-start) | async-done | bytes 2654240 | tf_op jit(solution)/shard_map/all_to_all | solution.py:171
  254.3 3.5 fusion.70
  257.8 4.2 fusion.1
  262.1 2.8 copy-done.2
  264.9 11.1 %fusion.12 = bf16[1152,128]{1,0:T(8,128)(2,1)} fusion(bf16[4608,128]{1,0:T(8,128)(2,1)S(1)} %bitcast.103, f32[1152,4608]{1,0:T(8,128)} %copy-done.2, f32[1152]{0:T(1024)S(1)} %get-tuple-element.30, f32[1152]{0:T(1024)S(1)} %fusion.1), kind=kOutput, calls=%fused_computation.14 | convolution fusion | flops 1369866240 | bytes 22717440 | tf_op jit(solution)/shard_map/dot_general | solution.py:187
  276.0 6.7 %all-to-all-start.1 = ((bf16[16,72,128]{2,1,0:T(8,128)(2,1)}), bf16[16,72,128]{2,1,0:T(8,128)(2,1)S(1)}, u32[]{:S(2)}, u32[]{:S(2)}) async-start(bf16[16,72,128]{2,1,0:T(8,128)(2,1)} %bitcast.28), calls=%async_computation.1 | async-start | bytes 589824 | tf_op jit(solution)/shard_map/all_to_all | solution.py:191
  283.0 54.5 %all-gather.14.cloned.1.call-done = bf16[768,3072]{0,1:T(8,128)(2,1)} async-done(((bf16[768,192]{0,1:T(8,128)(2,1)}), bf16[768,3072]{0,1:T(8,128)(2,1)}) %all-gather.14.cloned.1.call-update) | async-done | bytes 4718608 | tf_op jit(solution)/shard_map/all_gather | solution.py:200
  337.5 15.0 %fusion.29 = f32[576,3072]{1,0:T(8,128)} fusion(bf16[768,3072]{0,1:T(8,128)(2,1)} %all-gather.14.cloned.1.call-done, bf16[576,3072]{1,0:T(8,128)(2,1)} %bitcast.123, bf16[3072,768]{1,0:T(8,128)(2,1)} %all-gather.12.cloned.1.call-done), kind=kOutput, calls=%fused_computation.33 | convolution fusion | flops 5439799296 | bytes 20054016 | tf_op jit(solution)/shard_map/dot_general | solution.py:85
  352.7 46.0 %all-gather.10.cloned.1.call-done = bf16[256,3072]{0,1:T(8,128)(2,1)} async-done(((bf16[256,192]{0,1:T(8,128)(2,1)}), bf16[256,3072]{0,1:T(8,128)(2,1)}) %all-gather.10.cloned.1.call-update) | async-done | bytes 1572880 | tf_op jit(solution)/shard_map/all_gather | solution.py:199
  398.7 6.5 %add_convert_fusion = bf16[576,3072]{1,0:T(8,128)(2,1)} fusion(f32[576,3072]{1,0:T(8,128)} %fusion.29, bf16[256,3072]{0,1:T(8,128)(2,1)} %all-gather.10.cloned.1.call-done, bf16[72,8,2,128]{3,2,1,0:T(2,128)(2,1)S(1)} %bitcast.113), kind=kOutput, calls=%fused_computation.7 | convolution fusion | flops 909508608 | bytes 12484608 | tf_op jit(solution)/shard_map/dot_general | solution.py:84
  405.2 12.3 %copy.39 = bf16[2,288,3072]{1,0,2:T(2,128)(2,1)} copy(bf16[2,288,3072]{2,1,0:T(8,128)(2,1)} %bitcast.102) | data formatting | bytes 7077888
  417.5 10.2 %reshape.318 = bf16[3072,576]{1,0:T(8,128)(2,1)} reshape(bf16[3072,2,288]{2,1,0:T(2,128)(2,1)} %bitcast.101) | data formatting | bytes 7077888
  427.7 37.4 %reduce-scatter.4.cloned.1.call-done = bf16[384,576]{1,0:T(8,128)(2,1)} async-done(((bf16[3072,576]{1,0:T(8,128)(2,1)}), bf16[384,576]{1,0:T(8,128)(2,1)}) %reduce-scatter.4.cloned.1.call-update) | async-done | bytes 442384
  465.0 2.2 reshape.319
  468.1 0.8 slice_bitcast_fusion.2
  468.9 3.5 all-to-all-start.2
  473.0 5.2 %all-to-all-done.2 = bf16[2,1,256,384]{3,2,1,0:T(8,128)(2,1)S(1)} async-done(((bf16[2,1,256,384]{3,2,1,0:T(8,128)(2,1)}), bf16[2,1,256,384]{3,2,1,0:T(8,128)(2,1)S(1)}, u32[]{:S(2)}, u32[]{:S(2)}) %all-to-all-start.2) | async-done | bytes 393248 | tf_op jit(solution)/shard_map/all_to_all | solution.py:212
  478.3 1.0 multiply_add_fusion
  (62 shorter events, 11.8 us)
Async XLA Ops:
  7.2 2.3 copy-start
  7.2 84.7 %all-gather.8.cloned.1.call-start = ((), (), s32[]{:S(2)}) async-start(), calls=%async_computation.5 | async-start | bytes 5013504 | tf_op jit(solution)/shard_map/all_gather | solution.py:135
  7.9 120.0 %all-gather.6.cloned.1.call-start = ((), (), s32[]{:S(2)}) async-start(), calls=%async_computation.4 | async-start | bytes 3981312 | tf_op jit(solution)/shard_map/all_gather | solution.py:130
  74.5 208.5 %all-gather.12.cloned.1.call-start = ((), (), s32[]{:S(2)}) async-start(), calls=%async_computation.7 | async-start | bytes 5013504 | tf_op jit(solution)/shard_map/all_gather | solution.py:136
  75.2 262.3 %all-gather.14.cloned.1.call-start = ((), (), s32[]{:S(2)}) async-start(), calls=%async_computation.8 | async-start | bytes 5013504 | tf_op jit(solution)/shard_map/all_gather | solution.py:200
  142.0 10.8 %copy-start.5 = (s32[2]{0:T(128)S(1)}, s32[2]{0:T(128)}, u32[]{:S(2)}) copy-start(s32[2]{0:T(128)} %param.22) | copy-start | bytes 28
  142.0 112.2 %all-to-all-start = ((bf16[16,648,128]{2,1,0:T(8,128)(2,1)}), bf16[16,648,128]{2,1,0:T(8,128)(2,1)S(1)}, u32[]{:S(2)}, u32[]{:S(2)}) async-start(bf16[16,648,128]{2,1,0:T(8,128)(2,1)} %pad_maximum_fusion), calls=%async_computation | async-start | bytes 5308416 | tf_op jit(solution)/shard_map/all_to_all | solution.py:171
  152.1 246.6 %all-gather.10.cloned.1.call-start = ((), (), s32[]{:S(2)}) async-start(), calls=%async_computation.6 | async-start | bytes 1671168 | tf_op jit(solution)/shard_map/all_gather | solution.py:199
  257.8 7.1 %copy-start.2 = (f32[1152,4608]{1,0:T(8,128)}, f32[1152,4608]{1,0:T(8,128)S(1)}, u32[]{:S(2)}) copy-start(f32[1152,4608]{1,0:T(8,128)S(1)} %get-tuple-element.31) | copy-start | bytes 63700996
  276.0 76.5 %all-to-all-start.1 = ((bf16[16,72,128]{2,1,0:T(8,128)(2,1)}), bf16[16,72,128]{2,1,0:T(8,128)(2,1)S(1)}, u32[]{:S(2)}, u32[]{:S(2)}) async-start(bf16[16,72,128]{2,1,0:T(8,128)(2,1)} %bitcast.28), calls=%async_computation.1 | async-start | bytes 589824 | tf_op jit(solution)/shard_map/all_to_all | solution.py:191
  282.7 182.3 %reduce-scatter.4.cloned.1.call-start = ((), (), s32[]{:S(2)}) async-start(), calls=%async_computation.9 | async-start | bytes 4423680
  427.6 40.3 %copy-start.3 = (bf16[2,256,384]{2,1,0:T(8,128)(2,1)S(1)}, bf16[2,256,384]{2,1,0:T(8,128)(2,1)}, u32[]{:S(2)}) copy-start(bf16[2,256,384]{2,1,0:T(8,128)(2,1)} %param.13) | copy-start | bytes 1179652
  427.6 40.3 %copy-start.4 = (bf16[1,2,32,384]{3,2,1,0:T(8,128)(2,1)S(1)}, bf16[1,2,32,384]{3,2,1,0:T(8,128)(2,1)}, u32[]{:S(2)}) copy-start(bf16[1,2,32,384]{3,2,1,0:T(8,128)(2,1)} %param.12) | copy-start | bytes 147460
  465.0 14.2 %copy-start.1 = (bf16[192,3,384]{2,0,1:T(8,128)(2,1)S(1)}, bf16[192,3,384]{2,0,1:T(8,128)(2,1)}, u32[]{:S(2)}) copy-start(bf16[192,3,384]{2,0,1:T(8,128)(2,1)} %param.15) | copy-start | bytes 1327108
  468.9 9.3 %all-to-all-start.2 = ((bf16[2,1,256,384]{3,2,1,0:T(8,128)(2,1)}), bf16[2,1,256,384]{3,2,1,0:T(8,128)(2,1)S(1)}, u32[]{:S(2)}, u32[]{:S(2)}) async-start(bf16[2,1,256,384]{3,2,1,0:T(8,128)(2,1)} %slice_bitcast_fusion.2), calls=%async_computation.2 | async-start | bytes 786432 | tf_op jit(solution)/shard_map/all_to_all | solution.py:212
Sparse Core Ops, SparseCore 0:
  10.4 81.3 all-gather.7
  93.7 34.1 all-gather.5
  130.3 120.7 all-gather.11
  253.4 84.1 all-gather.13
  339.8 58.8 all-gather.9
  427.8 37.2 reduce-scatter.3
where the time goes:
time: 488 us; the launch traced here: 486 us
  waiting for transfers between devices  283 us (58%)
  blocking collectives  61.4 us (13%)
  local copies, waits for them, and re-layouts  47.1 us (10%)
  matrix products  43 us (9%)
  starting transfers between devices  20.9 us (4%)
  other arithmetic  15.6 us (3%)
  between operations  15.2 us (3%)
    all_to_all x1, waiting for transfers between devices, shards(): received = lax.all_to_all(send, 'seq', 0, 0, tiled=True)  100 us
    all_gather x1, waiting for transfers between devices, shards(): lax.all_gather(down_weight, 'seq', axis=1, tiled=True)  54.5 us
    psum x1, blocking collectives, shards(): modulation = lax.psum(mod_terms.reshape(3, dim_local), 'seq')  46.3 us
    all_gather x1, waiting for transfers between devices, shards(): lax.all_gather(attn_weight, 'seq', axis=1, tiled=True)  46 us
    unnamed x7, waiting for transfers between devices  39.6 us
    unnamed x16, local copies, waits for them, and re-layouts  28.2 us
    all_gather x1, waiting for transfers between devices, shards(): gathered = lax.all_gather(normed, 'wblk', axis=2, tiled=True)  23.6 us
    psum x1, blocking collectives, shards(): lax.psum((jnp.sum(hidden, axis=-1), jnp.sum(hidden * hidden, axis=-1)), '...  15.1 us
  transfers between devices with their start and end apart: 9, of which 7 were waited for; matrix products, arithmetic and copies ran while one was open for 14% of the time, Pallas kernels for 0%

commit v1 on v0

--- a/solution.py
+++ b/solution.py
@@ -127,7 +127,9 @@
     normed = (
         (hidden - average) * lax.rsqrt(variance + epsilon) * (1.0 + modulation[1]) + modulation[0]
     ).astype(jnp.bfloat16)
-    gathered = lax.all_gather(normed, "wblk", axis=2, tiled=True)
+    moved = jnp.stack([normed for _ in range(lax.axis_size("wblk"))], axis=0)
+    view_out = lax.all_to_all(moved, "wblk", 0, 0)
+    gathered = jnp.concatenate(view_out, axis=2)
     token_rows = gathered.reshape(row_count, D)
     projected, mlp_units = input_folder(
         token_rows,

time: 488 us -> 454 us (0.930)
  waiting for transfers between devices: 283 us -> 227 us
  local copies, waits for them, and re-layouts: 47.1 us -> 65.3 us
  starting transfers between devices: 20.9 us -> 26.4 us
    all_gather x1, waiting for transfers between devices: 54.5 us -> 0.02 us  [shards(): lax.all_gather(down_weight, 'seq', axis=1, tiled=True)]
    all_to_all x0 -> x1, waiting for transfers between devices: none -> 40.9 us  [shards(): view_out = lax.all_to_all(moved, 'wblk', 0, 0)]
    all_to_all x1, waiting for transfers between devices: 100 us -> 63.7 us  [shards(): received = lax.all_to_all(send, 'seq', 0, 0, tiled=True)]
    all_gather x1, waiting for transfers between devices: 0.02 us -> 35.3 us  [shards(): lax.all_gather(up_weight, 'seq', axis=0, tiled=True)]
    all_gather x1 -> x0, waiting for transfers between devices: 23.6 us -> none  [shards(): gathered = lax.all_gather(normed, 'wblk', axis=2, tiled=True)]
    all_gather x1, waiting for transfers between devices: 13.8 us -> 0.01 us  [shards(): lax.all_gather(qkv_weight, 'seq', axis=0, tiled=True)]
    dot_general x0 -> x1, local copies, waits for them, and re-layouts: none -> 6.61 us  [input_folder(): jnp.dot(source, pieces[0].reshape(width_rows, -1), preferred_element_type...]
    reshape x0 -> x1, local copies, waits for them, and re-layouts: none -> 5.9 us  [shards(): gathered = jnp.concatenate(view_out, axis=2)]
  transfers between devices with their start and end apart: 9 -> 9, of which waited for: 7 -> 6; matrix products, arithmetic and copies ran while one was open for 14% -> 19% of each run, Pallas kernels for 0% -> 0%
where the time goes in v1:
time: 454 us; the launch traced here: 453 us
  waiting for transfers between devices  227 us (50%)
  local copies, waits for them, and re-layouts  65.3 us (14%)
  blocking collectives  60.9 us (13%)
  matrix products  43.2 us (10%)
  starting transfers between devices  26.4 us (6%)
  other arithmetic  14.9 us (3%)
  between operations  14.9 us (3%)
    all_to_all x1, waiting for transfers between devices, shards(): received = lax.all_to_all(send, 'seq', 0, 0, tiled=True)  63.7 us
    psum x1, blocking collectives, shards(): modulation = lax.psum(mod_terms.reshape(3, dim_local), 'seq')  45.8 us
    all_gather x1, waiting for transfers between devices, shards(): lax.all_gather(attn_weight, 'seq', axis=1, tiled=True)  42.3 us
    all_to_all x1, waiting for transfers between devices, shards(): view_out = lax.all_to_all(moved, 'wblk', 0, 0)  40.9 us
    unnamed x6, waiting for transfers between devices  39.8 us
    all_gather x1, waiting for transfers between devices, shards(): lax.all_gather(up_weight, 'seq', axis=0, tiled=True)  35.3 us
    unnamed x21, local copies, waits for them, and re-layouts  32.8 us
    psum x1, blocking collectives, shards(): lax.psum((jnp.sum(hidden, axis=-1), jnp.sum(hidden * hidden, axis=-1)), '...  15.1 us
  transfers between devices with their start and end apart: 9, of which 6 were waited for; matrix products, arithmetic and copies ran while one was open for 19% of the time, Pallas kernels for 0%

profile of v1, /device:TPU:2, one launch (start us, length us, event | category | flops | bytes accessed | tf_op | source)
XLA Modules:
  0.0 452.7 jit_solution(3137220092038886451)
XLA Ops:
  10.4 1.3 convert_reduce_fusion
  11.7 15.1 %all-reduce.2 = (f32[2,288]{1,0:T(2,128)S(1)}, f32[2,288]{1,0:T(2,128)S(1)}) all-reduce(f32[2,288]{1,0:T(2,128)S(1)} %get-tuple-element.6, f32[2,288]{1,0:T(2,128)S(1)} %get-tuple-element.5), channel_id=1, replica_groups=mesh['cfg'=2,'seq'=16,'wblk'=8] {'wblk'}, use_global_device_ids=true, to_apply=%region_4.5 | all-reduce | flops 1152 | bytes 9216 | tf_op jit(solution)/shard_map/psum | solution.py:122
  26.8 45.8 %psum.21 = f32[3,384]{1,0:T(4,128)S(1)} all-reduce(f32[3,384]{1,0:T(4,128)S(1)} %bitcast.126), channel_id=1, replica_groups=mesh['cfg'=2,'seq'=16,'wblk'=8] {'seq'}, use_global_device_ids=true, to_apply=%region_0.1 | all-reduce | flops 1152 | bytes 9216 | tf_op jit(solution)/shard_map/psum | solution.py:119
  72.7 1.3 fusion.26
  74.0 2.2 stack.8
  76.2 4.6 %all-to-all-start = ((bf16[8,2,288,384]{3,2,1,0:T(8,128)(2,1)}), bf16[8,2,288,384]{3,2,1,0:T(8,128)(2,1)}, u32[]{:S(2)}, u32[]{:S(2)}) async-start(bf16[8,2,288,384]{3,2,1,0:T(8,128)(2,1)} %stack.8), calls=%async_computation | async-start | bytes 7077888 | tf_op jit(solution)/shard_map/all_to_all | solution.py:131
  82.6 40.9 %all-to-all-done = bf16[8,2,288,384]{3,2,1,0:T(8,128)(2,1)} async-done(((bf16[8,2,288,384]{3,2,1,0:T(8,128)(2,1)}), bf16[8,2,288,384]{3,2,1,0:T(8,128)(2,1)}, u32[]{:S(2)}, u32[]{:S(2)}) %all-to-all-start) | async-done | bytes 3538976 | tf_op jit(solution)/shard_map/all_to_all | solution.py:131
  123.5 5.9 %copy.37 = bf16[2,288,8,384]{3,2,1,0:T(8,128)(2,1)} copy(bf16[2,288,8,384]{3,1,0,2:T(8,128)(2,1)} %bitcast.6) | data formatting | bytes 7077888 | tf_op jit(solution)/shard_map/reshape | solution.py:132
  129.4 6.6 %reshape.324 = bf16[2,288,3072,1,1]{2,1,0,3,4:T(8,128)(2,1)} reshape(bf16[2,288,8,384]{3,2,1,0:T(8,128)(2,1)} %copy.37) | data formatting | bytes 7077888 | tf_op jit(solution)/shard_map/dot_general | solution.py:76
  136.0 12.6 %copy.49 = bf16[3072,3,2,128]{0,3,2,1:T(8,128)(2,1)} copy(bf16[3072,3,2,128]{3,2,1,0:T(2,128)(2,1)} %all-gather.5.cloned.1.call-done) | data formatting | bytes 9437184 | tf_op jit(solution)/shard_map/reshape | solution.py:77
  148.6 6.9 %fusion.6 = f32[2,288,3,2,128]{4,1,3,2,0:T(8,128)S(1)} fusion(bf16[3072,3,2,128]{0,3,2,1:T(8,128)(2,1)} %copy.49, bf16[2,288,3072,1,1]{2,1,0,3,4:T(8,128)(2,1)} %reshape.324), kind=kOutput, calls=%fused_computation.8 | convolution fusion | flops 2717908992 | bytes 10027008 | tf_op jit(solution)/shard_map/dot_general | solution.py:76
  157.8 0.8 subtract_convert_fusion.1
  161.1 1.7 pad_maximum_fusion
  162.7 9.3 %all-to-all-start.1 = ((bf16[16,648,128]{2,1,0:T(8,128)(2,1)}), bf16[16,648,128]{2,1,0:T(8,128)(2,1)S(1)}, u32[]{:S(2)}, u32[]{:S(2)}) async-start(bf16[16,648,128]{2,1,0:T(8,128)(2,1)} %pad_maximum_fusion), calls=%async_computation.1 | async-start | bytes 5308416 | tf_op jit(solution)/shard_map/all_to_all | solution.py:173
  173.9 4.6 %copy.55 = bf16[72,8,8,384]{3,1,2,0:T(8,128)(2,1)} copy(bf16[72,8,8,384]{3,2,1,0:T(8,128)(2,1)} %bitcast.104) | data formatting | bytes 7077888
  178.6 63.7 %all-to-all-done.1 = bf16[16,648,128]{2,1,0:T(8,128)(2,1)S(1)} async-done(((bf16[16,648,128]{2,1,0:T(8,128)(2,1)}), bf16[16,648,128]{2,1,0:T(8,128)(2,1)S(1)}, u32[]{:S(2)}, u32[]{:S(2)}) %all-to-all-start.1) | async-done | bytes 2654240 | tf_op jit(solution)/shard_map/all_to_all | solution.py:173
  242.4 3.5 fusion.70
  245.9 4.2 fusion.1
  250.2 2.8 copy-done.2
  253.0 11.2 %fusion.12 = bf16[1152,128]{1,0:T(8,128)(2,1)} fusion(bf16[4608,128]{1,0:T(8,128)(2,1)S(1)} %bitcast.107, f32[1152,4608]{1,0:T(8,128)} %copy-done.2, f32[1152]{0:T(1024)S(1)} %get-tuple-element.30, f32[1152]{0:T(1024)S(1)} %fusion.1), kind=kOutput, calls=%fused_computation.14 | convolution fusion | flops 1369866240 | bytes 22717440 | tf_op jit(solution)/shard_map/dot_general | solution.py:189
  264.2 8.3 %all-to-all-start.2 = ((bf16[16,72,128]{2,1,0:T(8,128)(2,1)}), bf16[16,72,128]{2,1,0:T(8,128)(2,1)S(1)}, u32[]{:S(2)}, u32[]{:S(2)}) async-start(bf16[16,72,128]{2,1,0:T(8,128)(2,1)} %bitcast.28), calls=%async_computation.2 | async-start | bytes 589824 | tf_op jit(solution)/shard_map/all_to_all | solution.py:193
  272.8 35.3 %all-gather.9.cloned.1.call-done = bf16[3072,768]{1,0:T(8,128)(2,1)} async-done(((bf16[192,768]{1,0:T(8,128)(2,1)}), bf16[3072,768]{1,0:T(8,128)(2,1)}) %all-gather.9.cloned.1.call-update) | async-done | bytes 4718608 | tf_op jit(solution)/shard_map/all_gather | solution.py:138
  308.1 15.0 %fusion.29 = f32[576,3072]{1,0:T(8,128)} fusion(bf16[768,3072]{0,1:T(8,128)(2,1)} %all-gather.11.cloned.1.call-done, bf16[576,3072]{1,0:T(8,128)(2,1)} %bitcast.111, bf16[3072,768]{1,0:T(8,128)(2,1)} %all-gather.9.cloned.1.call-done), kind=kOutput, calls=%fused_computation.33 | convolution fusion | flops 5439799296 | bytes 20054016 | tf_op jit(solution)/shard_map/dot_general | solution.py:85
  323.4 42.3 %all-gather.7.cloned.1.call-done = bf16[256,3072]{0,1:T(8,128)(2,1)} async-done(((bf16[256,192]{0,1:T(8,128)(2,1)}), bf16[256,3072]{0,1:T(8,128)(2,1)}) %all-gather.7.cloned.1.call-update) | async-done | bytes 1572880 | tf_op jit(solution)/shard_map/all_gather | solution.py:201
  365.7 6.5 %add_convert_fusion = bf16[576,3072]{1,0:T(8,128)(2,1)} fusion(f32[576,3072]{1,0:T(8,128)} %fusion.29, bf16[256,3072]{0,1:T(8,128)(2,1)} %all-gather.7.cloned.1.call-done, bf16[72,8,2,128]{3,2,1,0:T(2,128)(2,1)S(1)} %bitcast.118), kind=kOutput, calls=%fused_computation.7 | convolution fusion | flops 909508608 | bytes 12484608 | tf_op jit(solution)/shard_map/dot_general | solution.py:84
  372.2 12.3 %copy.50 = bf16[2,288,3072]{1,0,2:T(2,128)(2,1)} copy(bf16[2,288,3072]{2,1,0:T(8,128)(2,1)} %bitcast.106) | data formatting | bytes 7077888
  384.4 10.2 %reshape.327 = bf16[3072,576]{1,0:T(8,128)(2,1)} reshape(bf16[3072,2,288]{2,1,0:T(2,128)(2,1)} %bitcast.105) | data formatting | bytes 7077888
  394.6 37.4 %reduce-scatter.4.cloned.1.call-done = bf16[384,576]{1,0:T(8,128)(2,1)} async-done(((bf16[3072,576]{1,0:T(8,128)(2,1)}), bf16[384,576]{1,0:T(8,128)(2,1)}) %reduce-scatter.4.cloned.1.call-update) | async-done | bytes 442384
  432.0 2.2 reshape.328
  435.9 3.5 all-to-all-start.3
  440.0 5.2 %all-to-all-done.3 = bf16[2,1,256,384]{3,2,1,0:T(8,128)(2,1)S(1)} async-done(((bf16[2,1,256,384]{3,2,1,0:T(8,128)(2,1)}), bf16[2,1,256,384]{3,2,1,0:T(8,128)(2,1)S(1)}, u32[]{:S(2)}, u32[]{:S(2)}) %all-to-all-start.3) | async-done | bytes 393248 | tf_op jit(solution)/shard_map/all_to_all | solution.py:214
  445.2 1.0 multiply_add_fusion
  (69 shorter events, 13.8 us)
Async XLA Ops:
  7.2 3.1 copy-start
  7.2 128.8 %all-gather.5.cloned.1.call-start = ((), (), s32[]{:S(2)}) async-start(), calls=%async_computation.5 | async-start | bytes 5013504 | tf_op jit(solution)/shard_map/all_gather | solution.py:137
  7.9 264.9 %all-gather.11.cloned.1.call-start = ((), (), s32[]{:S(2)}) async-start(), calls=%async_computation.8 | async-start | bytes 5013504 | tf_op jit(solution)/shard_map/all_gather | solution.py:202
  76.2 5.4 %copy-start.5 = (f32[128]{0:T(128)S(1)}, f32[128]{0:T(128)}, u32[]{:S(2)}) copy-start(f32[128]{0:T(128)} %param.18) | copy-start | bytes 1540
  76.2 5.5 %copy-start.6 = (f32[128]{0:T(128)S(1)}, f32[128]{0:T(128)}, u32[]{:S(2)}) copy-start(f32[128]{0:T(128)} %param.19) | copy-start | bytes 1540
  76.2 47.3 %all-to-all-start = ((bf16[8,2,288,384]{3,2,1,0:T(8,128)(2,1)}), bf16[8,2,288,384]{3,2,1,0:T(8,128)(2,1)}, u32[]{:S(2)}, u32[]{:S(2)}) async-start(bf16[8,2,288,384]{3,2,1,0:T(8,128)(2,1)} %stack.8), calls=%async_computation | async-start | bytes 7077888 | tf_op jit(solution)/shard_map/all_to_all | solution.py:131
  80.9 227.3 %all-gather.9.cloned.1.call-start = ((), (), s32[]{:S(2)}) async-start(), calls=%async_computation.7 | async-start | bytes 5013504 | tf_op jit(solution)/shard_map/all_gather | solution.py:138
  162.7 9.9 %copy-start.7 = (s32[2]{0:T(128)S(1)}, s32[2]{0:T(128)}, u32[]{:S(2)}) copy-start(s32[2]{0:T(128)} %param.22) | copy-start | bytes 28
  162.7 79.5 %all-to-all-start.1 = ((bf16[16,648,128]{2,1,0:T(8,128)(2,1)}), bf16[16,648,128]{2,1,0:T(8,128)(2,1)S(1)}, u32[]{:S(2)}, u32[]{:S(2)}) async-start(bf16[16,648,128]{2,1,0:T(8,128)(2,1)} %pad_maximum_fusion), calls=%async_computation.1 | async-start | bytes 5308416 | tf_op jit(solution)/shard_map/all_to_all | solution.py:173
  172.0 193.7 %all-gather.7.cloned.1.call-start = ((), (), s32[]{:S(2)}) async-start(), calls=%async_computation.6 | async-start | bytes 1671168 | tf_op jit(solution)/shard_map/all_gather | solution.py:201
  245.9 7.1 %copy-start.2 = (f32[1152,4608]{1,0:T(8,128)}, f32[1152,4608]{1,0:T(8,128)S(1)}, u32[]{:S(2)}) copy-start(f32[1152,4608]{1,0:T(8,128)S(1)} %get-tuple-element.31) | copy-start | bytes 63700996
  264.2 59.0 %all-to-all-start.2 = ((bf16[16,72,128]{2,1,0:T(8,128)(2,1)}), bf16[16,72,128]{2,1,0:T(8,128)(2,1)S(1)}, u32[]{:S(2)}, u32[]{:S(2)}) async-start(bf16[16,72,128]{2,1,0:T(8,128)(2,1)} %bitcast.28), calls=%async_computation.2 | async-start | bytes 589824 | tf_op jit(solution)/shard_map/all_to_all | solution.py:193
  272.5 159.5 %reduce-scatter.4.cloned.1.call-start = ((), (), s32[]{:S(2)}) async-start(), calls=%async_computation.9 | async-start | bytes 4423680
  394.6 40.3 %copy-start.3 = (bf16[2,256,384]{2,1,0:T(8,128)(2,1)S(1)}, bf16[2,256,384]{2,1,0:T(8,128)(2,1)}, u32[]{:S(2)}) copy-start(bf16[2,256,384]{2,1,0:T(8,128)(2,1)} %param.13) | copy-start | bytes 1179652
  394.6 40.3 %copy-start.4 = (bf16[1,2,32,384]{3,2,1,0:T(8,128)(2,1)S(1)}, bf16[1,2,32,384]{3,2,1,0:T(8,128)(2,1)}, u32[]{:S(2)}) copy-start(bf16[1,2,32,384]{3,2,1,0:T(8,128)(2,1)} %param.12) | copy-start | bytes 147460
  432.0 14.2 %copy-start.1 = (bf16[192,3,384]{2,0,1:T(8,128)(2,1)S(1)}, bf16[192,3,384]{2,0,1:T(8,128)(2,1)}, u32[]{:S(2)}) copy-start(bf16[192,3,384]{2,0,1:T(8,128)(2,1)} %param.15) | copy-start | bytes 1327108
  435.9 9.3 %all-to-all-start.3 = ((bf16[2,1,256,384]{3,2,1,0:T(8,128)(2,1)}), bf16[2,1,256,384]{3,2,1,0:T(8,128)(2,1)S(1)}, u32[]{:S(2)}, u32[]{:S(2)}) async-start(bf16[2,1,256,384]{3,2,1,0:T(8,128)(2,1)} %slice_bitcast_fusion.2), calls=%async_computation.3 | async-start | bytes 786432 | tf_op jit(solution)/shard_map/all_to_all | solution.py:214
Sparse Core Ops, SparseCore 0:
  10.4 81.7 all-gather.4
  94.6 80.2 all-gather.10
  177.4 130.7 all-gather.8
  310.4 55.2 all-gather.6
  394.7 37.2 reduce-scatter.3
